TPU v7x, 32 devices: a whole 2x2x4 slice. The times are simulated.
32 devices in a mesh: rep: 2 (over y), seq: 4 (over z), head: 4 (over x, core).
Axes of the slice: x: 2, y: 2, z: 4, core: 2. Of those that a mesh axis runs over, the one named last changes fastest.
Arguments:
- queries: bfloat16 [3072, 2560], P(('rep', 'seq'), 'head'), parts along dimension 0, may hold values from -16 to 16
- keys: bfloat16 [3072, 2560], P(('rep', 'seq'), 'head'), parts along dimension 0, may hold values from -6 to 6
- values: bfloat16 [3072, 2560], P(('rep', 'seq'), 'head'), parts along dimension 0, may hold values from -6 to 6
- out_weight: bfloat16 [2560, 5120], P('seq', 'head'), may hold values from -0.3125 to 0.3125
- neighbours: int32 [8, 27], P('rep'), parts along dimension 0, may hold values from -1 to 3, as said below
- clip_ids: int32 [3072], P(('rep', 'seq')), parts along dimension 0, may hold values from 0 to 1
Outputs:
- output: bfloat16 [3072, 5120], P(('rep', 'seq'), 'head'), parts along dimension 0
There are 2 independent parts, one for each index of `rep`. A program takes and returns all parts, laid end to end along the dimension named above; an argument that names none is the same for every part. Nothing has to cross between parts.
Inputs may be any that keep to these rules, and one draw needn't show every extreme that they name: `neighbours`: column 9 (a + 1) + 3 (b + 1) + (c + 1) of row s, for a, b, c each -1, 0 or 1, is either -1 or s + a * 4 * 7 + b * 7 + c; column 13 of row s is s.
All inputs are finite; a program needn't handle non-finite values.
Results may differ from a plain program's by a relative error of at most 0.0058.
Values may be sent and summed in bfloat16 or wider, within the bound.
No kernel may reach another device: no remote copies, remote signals or barrier semaphores. Data moves between devices by JAX's collectives and lax.ppermute only.
A program may use at most 192 MiB of HBM per device.

v0:
```python
import math
import jax
import jax.numpy as jnp
from jax import lax
from jax.sharding import PartitionSpec as P

HD = 128
TGH = 4
TGW = 7


def from_behind(value, axis, by):
    peers = lax.axis_size(axis)
    pairs = [(i, i + by) for i in range(peers) if 0 <= i + by < peers]
    return lax.ppermute(value, axis, pairs)


def attend_head(query_head, key_head, value_head, allowed):
    scores = lax.dot_general(
        query_head, key_head, (((1,), (1,)), ((), ())), preferred_element_type=jnp.float32
    ) * (1.0 / math.sqrt(query_head.shape[1]))
    masked = jnp.where(allowed, scores, -1e30)
    highest = jnp.max(masked, axis=1, keepdims=True)
    raised = jnp.where(allowed, jnp.exp(masked - highest), 0.0)
    summed = jnp.sum(raised, axis=1, keepdims=True)
    weights = (raised / summed).astype(jnp.bfloat16)
    return jnp.dot(weights, value_head, preferred_element_type=jnp.float32).astype(jnp.bfloat16)


def on_device(queries, keys, values, out_weight, neighbours, clip_ids):
    tile_rows = queries.shape[0]
    feature_width = queries.shape[1]
    seq_count = lax.axis_size("seq")
    layer_tiles = TGH * TGW
    every_offset = set()
    for layer_step in (-1, 0, 1):
        for row_step in (-1, 0, 1):
            for col_step in (-1, 0, 1):
                every_offset.add(layer_step * layer_tiles + row_step * TGW + col_step)
    distances = [offset for offset in sorted(every_offset) if 0 < offset < seq_count]
    key_list = [keys]
    value_list = [values]
    clip_list = [clip_ids]
    offsets = [0]
    for distance in distances:
        below_keys, below_values, below_clips = from_behind(
            (keys, values, clip_ids), "seq", distance
        )
        above_keys, above_values, above_clips = from_behind(
            (keys, values, clip_ids), "seq", -distance
        )
        key_list += [below_keys, above_keys]
        value_list += [below_values, above_values]
        clip_list += [below_clips, above_clips]
        offsets += [distance, -distance]
    key_stack = jnp.stack(key_list)
    value_stack = jnp.stack(value_list)
    clip_stack = jnp.stack(clip_list)
    blocks = key_stack.shape[0]
    position = lax.axis_index("seq")
    window_row = lax.dynamic_index_in_dim(neighbours, position, 0, keepdims=False)
    sources = position - jnp.asarray(offsets, dtype=jnp.int32)
    present = jnp.any(
        (window_row[None, :] == sources[:, None]) & (window_row[None, :] >= 0), axis=1
    )
    key_clips = clip_stack.reshape(blocks * tile_rows)
    allowed = jnp.repeat(present, tile_rows)[None, :] & (clip_ids[:, None] == key_clips[None, :])
    key_rows = key_stack.reshape(blocks * tile_rows, feature_width)
    value_rows = value_stack.reshape(blocks * tile_rows, feature_width)
    head_outputs = []
    for head_index in range(feature_width // HD):
        first_col = head_index * HD
        head_outputs.append(
            attend_head(
                queries[:, first_col : first_col + HD],
                key_rows[:, first_col : first_col + HD],
                value_rows[:, first_col : first_col + HD],
                allowed,
            )
        )
    attended = jnp.concatenate(head_outputs, axis=1)
    all_features = lax.all_gather(attended, "head", axis=1, tiled=True)
    empty = jnp.zeros((tile_rows, out_weight.shape[1]), jnp.float32)
    weight_piece = lax.all_gather(out_weight, "seq", axis=0, tiled=True)
    features = lax.slice_in_dim(all_features, 0, weight_piece.shape[0], axis=1)
    projected = empty + jnp.dot(features, weight_piece, preferred_element_type=jnp.float32)
    return projected.astype(jnp.bfloat16)


def solution(mesh):
    in_specs = (
        P(("rep", "seq"), "head"),
        P(("rep", "seq"), "head"),
        P(("rep", "seq"), "head"),
        P("seq", "head"),
        P("rep", None),
        P(("rep", "seq")),
    )
    out_specs = P(("rep", "seq"), "head")
    return jax.shard_map(
        on_device, mesh=mesh, in_specs=in_specs, out_specs=out_specs, check_vma=False
    )
```

profile of v0, /device:TPU:0, one launch (start us, length us, event | category | flops | bytes accessed | tf_op | source)
XLA Modules:
  0.0 208.0 jit_solution(14518805611755408136)
XLA Ops:
  6.5 5.0 %collective-permute-start = (s32[384]{0:T(512)}, s32[384]{0:T(512)S(1)}, u32[]{:S(2)}, u32[]{:S(2)}) collective-permute-start(s32[384]{0:T(512)} %param.12), channel_id=1, source_target_pairs={{0,4},{4,8},{8,12},{1,5},{5,9},{9,13},{2,6},{6,10},{10,14},{3,7},{... | collective-permute-start | bytes 4616 | tf_op jit(solution)/shard_map/ppermute | solution.py:15
  11.6 1.3 collective-permute-start.1
  12.9 4.6 %collective-permute-start.2 = (bf16[384,640]{1,0:T(8,128)(2,1)}, bf16[384,640]{1,0:T(8,128)(2,1)S(1)}, u32[]{:S(2)}, u32[]{:S(2)}) collective-permute-start(bf16[384,640]{1,0:T(8,128)(2,1)} %param.8), channel_id=1, source_target_pairs={{0,4},{4,8},{8,12},{1,5},{5,9},{9,13},{2,6},{6,10},{10,14},{3,7},{... | collective-permute-start | bytes 1474568 | tf_op jit(solution)/shard_map/ppermute | solution.py:15
  17.5 1.3 collective-permute-start.3
  18.8 4.6 %collective-permute-start.4 = (bf16[384,640]{1,0:T(8,128)(2,1)}, bf16[384,640]{1,0:T(8,128)(2,1)S(1)}, u32[]{:S(2)}, u32[]{:S(2)}) collective-permute-start(bf16[384,640]{1,0:T(8,128)(2,1)} %param.9), channel_id=1, source_target_pairs={{0,4},{4,8},{8,12},{1,5},{5,9},{9,13},{2,6},{6,10},{10,14},{3,7},{... | collective-permute-start | bytes 1474568 | tf_op jit(solution)/shard_map/ppermute | solution.py:15
  23.4 0.7 compare_bitcast_fusion
  24.1 0.7 fusion.35
  25.6 0.7 stack.36
  26.4 1.3 collective-permute-start.5
  27.8 1.7 collective-permute-done.2
  29.4 4.3 %collective-permute-done.3 = bf16[384,640]{1,0:T(8,128)(2,1)S(1)} collective-permute-done((bf16[384,640]{1,0:T(8,128)(2,1)}, bf16[384,640]{1,0:T(8,128)(2,1)S(1)}, u32[]{:S(2)}, u32[]{:S(2)}) %collective-permute-start.3) | collective-permute-done | bytes 491552 | tf_op jit(solution)/shard_map/ppermute | solution.py:15
  33.8 1.2 pad_maximum_fusion
  38.2 4.0 %collective-permute-done.5 = bf16[384,640]{1,0:T(8,128)(2,1)S(1)} collective-permute-done((bf16[384,640]{1,0:T(8,128)(2,1)}, bf16[384,640]{1,0:T(8,128)(2,1)S(1)}, u32[]{:S(2)}, u32[]{:S(2)}) %collective-permute-start.5) | collective-permute-done | bytes 491552 | tf_op jit(solution)/shard_map/ppermute | solution.py:15
  42.4 2.3 %fusion.14 = (f32[384]{0:T(512)S(1)}, f32[384]{0:T(512)S(1)}, f32[384]{0:T(512)S(1)}, f32[384]{0:T(512)S(1)}, f32[384]{0:T(512)S(1)}) fusion(f32[384,1152]{0,1:T(8,128)S(1)} %get-tuple-element.11, f32[384]{0:T(512)S(1)} %get-tuple-element.10, s32[384]{0:T(512)S(1)} %copy-done.2, s32[1152]{0:T(1024)S(1)} %eq.35, pred[1152]{0:T(1024)(128)(4,1)S(1)} %and.24, ...), kind=kLoop, calls=%fused_computation.33 | loop fusion | flops 7518336 | bytes 8870016 | tf_op jit(solution)/shard_map/reduce_sum | solution.py:25
  44.7 1.0 fusion.15
  45.7 1.0 fusion.16
  46.8 1.0 fusion.17
  47.8 1.0 fusion.18
  48.8 1.0 fusion.19
  49.8 0.8 copy-done.1
  50.7 0.7 all-gather.5.cloned.1.call-update
  51.4 21.5 %all-gather.3.cloned.1.call-done = bf16[384,2560]{1,0:T(8,128)(2,1)} async-done(((bf16[384,640]{1,0:T(8,128)(2,1)}), bf16[384,2560]{1,0:T(8,128)(2,1)}) %all-gather.3.cloned.1.call-update) | async-done | bytes 1966096 | tf_op jit(solution)/shard_map/all_gather | solution.py:82
  72.8 121.2 %all-gather.5.cloned.1.call-done = bf16[2560,1280]{1,0:T(8,128)(2,1)} async-done(((bf16[640,1280]{1,0:T(8,128)(2,1)}), bf16[2560,1280]{1,0:T(8,128)(2,1)}) %all-gather.5.cloned.1.call-update) | async-done | bytes 6553616 | tf_op jit(solution)/shard_map/all_gather | solution.py:84
  194.1 7.1 %convolution_convert_fusion = bf16[384,1280]{1,0:T(8,128)(2,1)} fusion(bf16[384,2560]{1,0:T(8,128)(2,1)} %all-gather.3.cloned.1.call-done, bf16[2560,1280]{1,0:T(8,128)(2,1)} %all-gather.5.cloned.1.call-done), kind=kOutput, calls=%fused_computation.15 | convolution fusion | flops 2517073920 | bytes 9502720 | tf_op jit(solution)/shard_map/dot_general | solution.py:86
  (27 shorter events, 4.4 us)
Async XLA Ops:
  6.5 28.4 %copy-start.2 = (s32[384]{0:T(512)S(1)}, s32[384]{0:T(512)}, u32[]{:S(2)}) copy-start(s32[384]{0:T(512)} %param.12) | copy-start | bytes 4612
  6.5 28.5 %copy-start.3 = (bf16[384,640]{1,0:T(8,128)(2,1)S(1)}, bf16[384,640]{1,0:T(8,128)(2,1)}, u32[]{:S(2)}) copy-start(bf16[384,640]{1,0:T(8,128)(2,1)} %param.7) | copy-start | bytes 1474564
  6.5 66.3 %all-gather.3.cloned.1.call-start = ((), (), s32[]{:S(2)}) async-start(), calls=%async_computation | async-start | bytes 2457600 | tf_op jit(solution)/shard_map/all_gather | solution.py:82
  6.5 19.8 %collective-permute-start = (s32[384]{0:T(512)}, s32[384]{0:T(512)S(1)}, u32[]{:S(2)}, u32[]{:S(2)}) collective-permute-start(s32[384]{0:T(512)} %param.12), channel_id=1, source_target_pairs={{0,4},{4,8},{8,12},{1,5},{5,9},{9,13},{2,6},{6,10},{10,14},{3,7},{... | collective-permute-start | bytes 4616 | tf_op jit(solution)/shard_map/ppermute | solution.py:15
  11.6 16.1 %collective-permute-start.1 = (s32[384]{0:T(512)}, s32[384]{0:T(512)S(1)}, u32[]{:S(2)}, u32[]{:S(2)}) collective-permute-start(s32[384]{0:T(512)} %param.12), channel_id=1, source_target_pairs={{4,0},{8,4},{12,8},{5,1},{9,5},{13,9},{6,2},{10,6},{14,10},{7,3},{... | collective-permute-start | bytes 4616 | tf_op jit(solution)/shard_map/ppermute | solution.py:15
  12.9 16.5 %collective-permute-start.2 = (bf16[384,640]{1,0:T(8,128)(2,1)}, bf16[384,640]{1,0:T(8,128)(2,1)S(1)}, u32[]{:S(2)}, u32[]{:S(2)}) collective-permute-start(bf16[384,640]{1,0:T(8,128)(2,1)} %param.8), channel_id=1, source_target_pairs={{0,4},{4,8},{8,12},{1,5},{5,9},{9,13},{2,6},{6,10},{10,14},{3,7},{... | collective-permute-start | bytes 1474568 | tf_op jit(solution)/shard_map/ppermute | solution.py:15
  17.5 16.3 %collective-permute-start.3 = (bf16[384,640]{1,0:T(8,128)(2,1)}, bf16[384,640]{1,0:T(8,128)(2,1)S(1)}, u32[]{:S(2)}, u32[]{:S(2)}) collective-permute-start(bf16[384,640]{1,0:T(8,128)(2,1)} %param.8), channel_id=1, source_target_pairs={{4,0},{8,4},{12,8},{5,1},{9,5},{13,9},{6,2},{10,6},{14,10},{7,3},{... | collective-permute-start | bytes 1474568 | tf_op jit(solution)/shard_map/ppermute | solution.py:15
  18.8 19.4 %collective-permute-start.4 = (bf16[384,640]{1,0:T(8,128)(2,1)}, bf16[384,640]{1,0:T(8,128)(2,1)S(1)}, u32[]{:S(2)}, u32[]{:S(2)}) collective-permute-start(bf16[384,640]{1,0:T(8,128)(2,1)} %param.9), channel_id=1, source_target_pairs={{0,4},{4,8},{8,12},{1,5},{5,9},{9,13},{2,6},{6,10},{10,14},{3,7},{... | collective-permute-start | bytes 1474568 | tf_op jit(solution)/shard_map/ppermute | solution.py:15
  26.4 15.9 %collective-permute-start.5 = (bf16[384,640]{1,0:T(8,128)(2,1)}, bf16[384,640]{1,0:T(8,128)(2,1)S(1)}, u32[]{:S(2)}, u32[]{:S(2)}) collective-permute-start(bf16[384,640]{1,0:T(8,128)(2,1)} %param.9), channel_id=1, source_target_pairs={{4,0},{8,4},{12,8},{5,1},{9,5},{13,9},{6,2},{10,6},{14,10},{7,3},{... | collective-permute-start | bytes 1474568 | tf_op jit(solution)/shard_map/ppermute | solution.py:15
  37.5 4.7 %copy-start = (bf16[384,640]{1,0:T(8,128)(2,1)S(1)}, bf16[384,640]{1,0:T(8,128)(2,1)}, u32[]{:S(2)}) copy-start(bf16[384,640]{1,0:T(8,128)(2,1)} %param.9) | copy-start | bytes 1474564
  49.8 0.8 copy-start.1
  50.6 143.4 %all-gather.5.cloned.1.call-start = ((), (), s32[]{:S(2)}) async-start(), calls=%async_computation.1 | async-start | bytes 8192000 | tf_op jit(solution)/shard_map/all_gather | solution.py:84
Sparse Core Ops, SparseCore 0:
  50.7 22.0 all-gather.2
  74.4 119.6 all-gather.4
where the time goes:
time: 208 us
  waiting for transfers between devices  154 us (74%)
  starting transfers between devices  18.1 us (9%)
  matrix products  15.3 us (7%)
  between operations  13.6 us (7%)
  other arithmetic  5.25 us (3%)
  local copies, waits for them, and re-layouts  2.27 us (1%)
    all_gather x1, waiting for transfers between devices, on_device(): weight_piece = lax.all_gather(out_weight, 'seq', axis=0, tiled=True)  121 us
    all_gather x1, waiting for transfers between devices, on_device(): all_features = lax.all_gather(attended, 'head', axis=1, tiled=True)  21.5 us
    ppermute x6, starting transfers between devices, from_behind(): return lax.ppermute(value, axis, pairs)  18.1 us
    ppermute x6, waiting for transfers between devices, from_behind(): return lax.ppermute(value, axis, pairs)  10.1 us
    dot_general x1, matrix products, on_device(): jnp.dot(features, weight_piece, preferred_element_type=jnp.float32)  7.1 us
    dot_general x5, matrix products, attend_head(): jnp.dot(weights, value_head, preferred_element_type=jnp.float32)  5.04 us
  transfers between devices with their start and end apart: 8, of which 6 were waited for; matrix products, arithmetic and copies ran while one was open for 4% of the time, Pallas kernels for 0%

commit v1 on v0

--- a/solution.py
+++ b/solution.py
@@ -79,7 +79,15 @@
             )
         )
     attended = jnp.concatenate(head_outputs, axis=1)
-    all_features = lax.all_gather(attended, "head", axis=1, tiled=True)
+    ways, here = (lax.axis_size("head"), lax.axis_index("head"))
+    grown, reach = (attended, 1)
+    while reach < ways:
+        theirs = lax.ppermute(grown, "head", [(d, d ^ reach) for d in range(ways)])
+        mine_first = jnp.concatenate([grown, theirs], axis=1)
+        theirs_first = jnp.concatenate([theirs, grown], axis=1)
+        grown = jnp.where(here & reach == 0, mine_first, theirs_first)
+        reach = 2 * reach
+    all_features = grown
     empty = jnp.zeros((tile_rows, out_weight.shape[1]), jnp.float32)
     weight_piece = lax.all_gather(out_weight, "seq", axis=0, tiled=True)
     features = lax.slice_in_dim(all_features, 0, weight_piece.shape[0], axis=1)

time: 208 us -> 159 us (0.76)
  waiting for transfers between devices: 154 us -> 104 us
    all_gather x1, waiting for transfers between devices: 121 us -> 39.1 us  [on_device(): weight_piece = lax.all_gather(out_weight, 'seq', axis=0, tiled=True)]
    ppermute x6, waiting for transfers between devices: 10.1 us -> 39.6 us  [from_behind(): return lax.ppermute(value, axis, pairs)]
    ppermute x0 -> x2, waiting for transfers between devices: none -> 24.1 us  [on_device(): theirs = lax.ppermute(grown, 'head', [(d, d ^ reach) for d in range(ways)])]
    all_gather x1 -> x0, waiting for transfers between devices: 21.5 us -> none  [on_device(): all_features = lax.all_gather(attended, 'head', axis=1, tiled=True)]
  transfers between devices with their start and end apart: 8 -> 9, of which waited for: 6 -> 5; matrix products, arithmetic and copies ran while one was open for 4% -> 9% of each run, Pallas kernels for 0% -> 0%
where the time goes in v1:
time: 159 us; the launch traced here: 158 us
  waiting for transfers between devices  104 us (65%)
  starting transfers between devices  19.7 us (12%)
  matrix products  14.4 us (9%)
  between operations  13.6 us (9%)
  other arithmetic  4.34 us (3%)
  local copies, waits for them, and re-layouts  2.5 us (2%)
    ppermute x6, waiting for transfers between devices, from_behind(): return lax.ppermute(value, axis, pairs)  39.6 us
    all_gather x1, waiting for transfers between devices, on_device(): weight_piece = lax.all_gather(out_weight, 'seq', axis=0, tiled=True)  39.1 us
    ppermute x2, waiting for transfers between devices, on_device(): theirs = lax.ppermute(grown, 'head', [(d, d ^ reach) for d in range(ways)])  24.1 us
    ppermute x6, starting transfers between devices, from_behind(): return lax.ppermute(value, axis, pairs)  18.1 us
    dot_general x1, matrix products, on_device(): jnp.dot(features, weight_piece, preferred_element_type=jnp.float32)  6.62 us
    dot_general x5, matrix products, attend_head(): jnp.dot(weights, value_head, preferred_element_type=jnp.float32)  4.64 us
  transfers between devices with their start and end apart: 9, of which 5 were waited for; matrix products, arithmetic and copies ran while one was open for 9% of the time, Pallas kernels for 0%

profile of v1, /device:TPU:0, one launch (start us, length us, event | category | flops | bytes accessed | tf_op | source)
XLA Modules:
  0.0 158.2 jit_solution(14815643945886860622)
XLA Ops:
  6.5 0.7 all-gather.2.cloned.1.call-update
  7.3 5.1 %collective-permute-start.2 = (bf16[384,640]{1,0:T(8,128)(2,1)}, bf16[384,640]{1,0:T(8,128)(2,1)S(1)}, u32[]{:S(2)}, u32[]{:S(2)}) collective-permute-start(bf16[384,640]{1,0:T(8,128)(2,1)} %param.8), channel_id=1, source_target_pairs={{0,4},{4,8},{8,12},{1,5},{5,9},{9,13},{2,6},{6,10},{10,14},{3,7},{... | collective-permute-start | bytes 1474568 | tf_op jit(solution)/shard_map/ppermute | solution.py:15
  12.4 1.3 collective-permute-start.3
  13.7 4.6 %collective-permute-start.4 = (bf16[384,640]{1,0:T(8,128)(2,1)}, bf16[384,640]{1,0:T(8,128)(2,1)S(1)}, u32[]{:S(2)}, u32[]{:S(2)}) collective-permute-start(bf16[384,640]{1,0:T(8,128)(2,1)} %param.9), channel_id=1, source_target_pairs={{0,4},{4,8},{8,12},{1,5},{5,9},{9,13},{2,6},{6,10},{10,14},{3,7},{... | collective-permute-start | bytes 1474568 | tf_op jit(solution)/shard_map/ppermute | solution.py:15
  18.2 1.3 collective-permute-start.5
  19.5 4.5 %collective-permute-start = (s32[384]{0:T(512)}, s32[384]{0:T(512)S(1)}, u32[]{:S(2)}, u32[]{:S(2)}) collective-permute-start(s32[384]{0:T(512)} %param.12), channel_id=1, source_target_pairs={{0,4},{4,8},{8,12},{1,5},{5,9},{9,13},{2,6},{6,10},{10,14},{3,7},{... | collective-permute-start | bytes 4616 | tf_op jit(solution)/shard_map/ppermute | solution.py:15
  24.1 0.7 broadcast_add_fusion
  24.8 0.7 compare_bitcast_fusion
  25.5 0.7 fusion.36
  26.1 21.0 %collective-permute-done = s32[384]{0:T(512)S(1)} collective-permute-done((s32[384]{0:T(512)}, s32[384]{0:T(512)S(1)}, u32[]{:S(2)}, u32[]{:S(2)}) %collective-permute-start) | collective-permute-done | bytes 1568 | tf_op jit(solution)/shard_map/ppermute | solution.py:15
  47.1 1.3 collective-permute-start.1
  48.6 0.7 stack.36
  49.4 18.6 %collective-permute-done.1 = s32[384]{0:T(512)S(1)} collective-permute-done((s32[384]{0:T(512)}, s32[384]{0:T(512)S(1)}, u32[]{:S(2)}, u32[]{:S(2)}) %collective-permute-start.1) | collective-permute-done | bytes 1568 | tf_op jit(solution)/shard_map/ppermute | solution.py:15
  72.5 2.3 %fusion.20 = (f32[384]{0:T(512)S(1)}, f32[384]{0:T(512)S(1)}, f32[384]{0:T(512)S(1)}, f32[384]{0:T(512)S(1)}, f32[384]{0:T(512)S(1)}) fusion(f32[384,1152]{0,1:T(8,128)S(1)} %get-tuple-element.23, f32[384]{0:T(512)S(1)} %get-tuple-element.22, s32[384]{0:T(512)S(1)} %copy-done.2, s32[1152]{0:T(1024)S(1)} %eq.43, pred[1152]{0:T(1024)(128)(4,1)S(1)} %and.33, ...), kind=kLoop, calls=%fused_computation.40 | loop fusion | flops 7518336 | bytes 8870016 | tf_op jit(solution)/shard_map/reduce_sum | solution.py:25
  74.8 0.9 constant_dynamic-update-slice_fusion.4
  75.7 0.9 constant_dynamic-update-slice_fusion.3
  76.6 0.9 constant_dynamic-update-slice_fusion.2
  77.6 0.9 constant_dynamic-update-slice_fusion.1
  78.5 0.9 constant_dynamic-update-slice_fusion
  79.5 1.8 %collective-permute-done.6 = bf16[384,640]{0,1:T(8,128)(2,1)S(1)} collective-permute-done((bf16[384,640]{0,1:T(8,128)(2,1)S(1)}, bf16[384,640]{0,1:T(8,128)(2,1)S(1)}, u32[]{:S(2)}, u32[]{:S(2)}) %collective-permute-start.6) | collective-permute-done | bytes 491552 | tf_op jit(solution)/shard_map/ppermute | solution.py:85
  81.7 1.6 collective-permute-start.7
  83.3 22.3 %collective-permute-done.7 = bf16[384,1280]{0,1:T(8,128)(2,1)S(1)} collective-permute-done((bf16[384,1280]{0,1:T(8,128)(2,1)S(1)}, bf16[384,1280]{0,1:T(8,128)(2,1)S(1)}, u32[]{:S(2)}, u32[]{:S(2)}) %collective-permute-start.7) | collective-permute-done | bytes 983072 | tf_op jit(solution)/shard_map/ppermute | solution.py:85
  105.6 39.1 %all-gather.2.cloned.1.call-done = bf16[2560,1280]{1,0:T(8,128)(2,1)} async-done(((bf16[640,1280]{1,0:T(8,128)(2,1)}), bf16[2560,1280]{1,0:T(8,128)(2,1)}) %all-gather.2.cloned.1.call-update) | async-done | bytes 6553616 | tf_op jit(solution)/shard_map/all_gather | solution.py:92
  144.7 6.6 %convolution_convert_fusion = bf16[384,1280]{1,0:T(8,128)(2,1)} fusion(bf16[2560,1280]{1,0:T(8,128)(2,1)} %all-gather.2.cloned.1.call-done, bf16[384,1280]{0,1:T(8,128)(2,1)S(1)} %collective-permute-done.7, bf16[384,1280]{0,1:T(8,128)(2,1)S(1)} %broadcast_select_fusion, pred[]{:T(512)S(6)} %eq.36), kind=kOutput, calls=%fused_computation.15 | convolution fusion | flops 2525921280 | bytes 9502721 | tf_op jit(solution)/shard_map/dot_general | solution.py:94
  (35 shorter events, 5.1 us)
Async XLA Ops:
  6.5 61.5 %copy-start = (bf16[384,640]{1,0:T(8,128)(2,1)S(1)}, bf16[384,640]{1,0:T(8,128)(2,1)}, u32[]{:S(2)}) copy-start(bf16[384,640]{1,0:T(8,128)(2,1)} %param.8) | copy-start | bytes 1474564
  6.5 138.2 %all-gather.2.cloned.1.call-start = ((), (), s32[]{:S(2)}) async-start(), calls=%async_computation | async-start | bytes 8192000 | tf_op jit(solution)/shard_map/all_gather | solution.py:92
  7.3 61.0 %copy-start.1 = (bf16[384,640]{1,0:T(8,128)(2,1)S(1)}, bf16[384,640]{1,0:T(8,128)(2,1)}, u32[]{:S(2)}) copy-start(bf16[384,640]{1,0:T(8,128)(2,1)} %param.9) | copy-start | bytes 1474564
  7.3 60.8 %collective-permute-start.2 = (bf16[384,640]{1,0:T(8,128)(2,1)}, bf16[384,640]{1,0:T(8,128)(2,1)S(1)}, u32[]{:S(2)}, u32[]{:S(2)}) collective-permute-start(bf16[384,640]{1,0:T(8,128)(2,1)} %param.8), channel_id=1, source_target_pairs={{0,4},{4,8},{8,12},{1,5},{5,9},{9,13},{2,6},{6,10},{10,14},{3,7},{... | collective-permute-start | bytes 1474568 | tf_op jit(solution)/shard_map/ppermute | solution.py:15
  12.4 55.7 %collective-permute-start.3 = (bf16[384,640]{1,0:T(8,128)(2,1)}, bf16[384,640]{1,0:T(8,128)(2,1)S(1)}, u32[]{:S(2)}, u32[]{:S(2)}) collective-permute-start(bf16[384,640]{1,0:T(8,128)(2,1)} %param.8), channel_id=1, source_target_pairs={{4,0},{8,4},{12,8},{5,1},{9,5},{13,9},{6,2},{10,6},{14,10},{7,3},{... | collective-permute-start | bytes 1474568 | tf_op jit(solution)/shard_map/ppermute | solution.py:15
  13.7 54.6 %collective-permute-start.4 = (bf16[384,640]{1,0:T(8,128)(2,1)}, bf16[384,640]{1,0:T(8,128)(2,1)S(1)}, u32[]{:S(2)}, u32[]{:S(2)}) collective-permute-start(bf16[384,640]{1,0:T(8,128)(2,1)} %param.9), channel_id=1, source_target_pairs={{0,4},{4,8},{8,12},{1,5},{5,9},{9,13},{2,6},{6,10},{10,14},{3,7},{... | collective-permute-start | bytes 1474568 | tf_op jit(solution)/shard_map/ppermute | solution.py:15
  18.2 50.0 %collective-permute-start.5 = (bf16[384,640]{1,0:T(8,128)(2,1)}, bf16[384,640]{1,0:T(8,128)(2,1)S(1)}, u32[]{:S(2)}, u32[]{:S(2)}) collective-permute-start(bf16[384,640]{1,0:T(8,128)(2,1)} %param.9), channel_id=1, source_target_pairs={{4,0},{8,4},{12,8},{5,1},{9,5},{13,9},{6,2},{10,6},{14,10},{7,3},{... | collective-permute-start | bytes 1474568 | tf_op jit(solution)/shard_map/ppermute | solution.py:15
  19.5 27.6 %collective-permute-start = (s32[384]{0:T(512)}, s32[384]{0:T(512)S(1)}, u32[]{:S(2)}, u32[]{:S(2)}) collective-permute-start(s32[384]{0:T(512)} %param.12), channel_id=1, source_target_pairs={{0,4},{4,8},{8,12},{1,5},{5,9},{9,13},{2,6},{6,10},{10,14},{3,7},{... | collective-permute-start | bytes 4616 | tf_op jit(solution)/shard_map/ppermute | solution.py:15
  47.1 20.9 %collective-permute-start.1 = (s32[384]{0:T(512)}, s32[384]{0:T(512)S(1)}, u32[]{:S(2)}, u32[]{:S(2)}) collective-permute-start(s32[384]{0:T(512)} %param.12), channel_id=1, source_target_pairs={{4,0},{8,4},{12,8},{5,1},{9,5},{13,9},{6,2},{10,6},{14,10},{7,3},{... | collective-permute-start | bytes 4616 | tf_op jit(solution)/shard_map/ppermute | solution.py:15
  68.2 0.7 copy-start.2
  68.3 1.0 copy-start.3
  79.4 1.9 %collective-permute-start.6 = (bf16[384,640]{0,1:T(8,128)(2,1)S(1)}, bf16[384,640]{0,1:T(8,128)(2,1)S(1)}, u32[]{:S(2)}, u32[]{:S(2)}) collective-permute-start(bf16[384,640]{0,1:T(8,128)(2,1)S(1)} %get-tuple-element.12), channel_id=1, source_target_pairs={{0,1},{1,0},{2,3},{3,2},{4,5},{5,4},{6,7},{7,6},{8,9},{9,8},{10,11... | collective-permute-start | bytes 1474568 | tf_op jit(solution)/shard_map/ppermute | solution.py:85
  81.7 23.9 %collective-permute-start.7 = (bf16[384,1280]{0,1:T(8,128)(2,1)S(1)}, bf16[384,1280]{0,1:T(8,128)(2,1)S(1)}, u32[]{:S(2)}, u32[]{:S(2)}) collective-permute-start(bf16[384,1280]{0,1:T(8,128)(2,1)S(1)} %broadcast_select_fusion), channel_id=1, source_target_pairs={{0,2},{1,3},{2,0},{3,1},{4,6},{5,7},{6,4},{7,5},{8,10},{9,11},{10,... | collective-permute-start | bytes 2949128 | tf_op jit(solution)/shard_map/ppermute | solution.py:85
Sparse Core Ops, SparseCore 0:
  8.9 135.7 all-gather.1
